TPU v7x, 256 devices: a whole 4x4x8 slice. The times are simulated.
256 devices in a mesh: vgrp: 4 (over y), samp: 64 (over z, x, core).
Axes of the slice: x: 4, y: 4, z: 8, core: 2. Of those that a mesh axis runs over, the one named last changes fastest.
Arguments:
- phenotype: float32 [196608], P(('vgrp', 'samp')), may hold values from -6 to 6
- exposures: float32 [196608, 128], P('samp'), may hold values from -6 to 6
- perms: int32 [16, 196608], P(None, 'samp'), may hold values from 0 to 196607, each once within a row
- genotypes: int32 [196608, 2048], P('samp', 'vgrp'), may hold values from 0 to 2
Outputs:
- statistics: float32 [2048, 16], P(('vgrp', 'samp'))
Inputs may be any that keep to these rules, and one draw needn't show every extreme that they name: Each row of perms holds every sample index once.
All inputs are finite; a program needn't handle non-finite values.
Results may differ from a plain program's by a relative error of at most 0.00075.
Values sent between devices are 32-bit elements; how exact they have to be, the bound alone decides.
No kernel may reach another device: no remote copies, remote signals or barrier semaphores. Data moves between devices by JAX's collectives and lax.ppermute only.
A program may use at most 64 MiB of HBM per device.

v0:
```python
import jax
import jax.numpy as jnp
from jax import lax
from jax.sharding import PartitionSpec as P


def chol_solve(factor, rhs):
    middle = lax.linalg.triangular_solve(factor, rhs, left_side=True, lower=True)
    return lax.linalg.triangular_solve(factor, middle, left_side=True, lower=True, transpose_a=True)


def per_device(phenotype, exposures, perms, genotypes):
    hi = lax.Precision.HIGHEST
    nv = lax.axis_size("vgrp")
    local_rows = exposures.shape[0]
    width = exposures.shape[1]
    quarter = local_rows // nv
    offset_rows = lax.axis_index("vgrp") * quarter
    expo_part = lax.dynamic_slice_in_dim(exposures, offset_rows, quarter, 0)
    gram_part = jnp.dot(expo_part.T, expo_part, precision=hi)
    gram = lax.psum(gram_part, ("vgrp", "samp"))
    pheno_full = lax.all_gather(phenotype, ("vgrp", "samp"), axis=0, tiled=True)
    samples = pheno_full.shape[0]
    system = gram + 0.5 * samples * jnp.eye(width, dtype=jnp.float32)
    factor = jnp.linalg.cholesky(system)
    perm_part = lax.dynamic_slice_in_dim(perms, offset_rows, quarter, 1)
    pheno_part = jnp.take(pheno_full, perm_part.T, axis=0, mode="clip")
    cross_part = jnp.dot(expo_part.T, pheno_part, precision=hi)
    cross = lax.psum(cross_part, ("vgrp", "samp"))
    coefficients = chol_solve(factor, cross)
    permuted = lax.all_gather(pheno_part, "vgrp", axis=0, tiled=True)
    residuals = permuted - jnp.dot(exposures, coefficients, precision=hi)
    nperm = residuals.shape[1]
    weighted = (
        (exposures[:, :, None] * residuals[:, None, :])
        .reshape(local_rows, width * nperm)
        .astype(jnp.bfloat16)
    )
    dosages = genotypes.astype(jnp.bfloat16)
    partial = jnp.dot(dosages.T, weighted, preferred_element_type=jnp.float32)
    own_scores = lax.psum_scatter(partial, "samp", scatter_dimension=0, tiled=True)
    own_rows = own_scores.shape[0]
    shaped = own_scores.reshape(own_rows, width, nperm)
    return jnp.sum(shaped * shaped, axis=1) / (samples * width)


def solution(mesh):
    return jax.shard_map(
        per_device,
        mesh=mesh,
        in_specs=(P(("vgrp", "samp")), P("samp", None), P(None, "samp"), P("samp", "vgrp")),
        out_specs=P(("vgrp", "samp"), None),
        check_vma=False,
    )
```

profile of v0, /device:TPU:8, one launch (start us, length us, event | category | flops | bytes accessed | tf_op | source)
XLA Modules:
  0.0 509.8 jit_solution(5372724521363424822)
XLA Ops:
  6.5 2.6 fusion.4
  9.6 0.7 reshape.31
  10.3 77.2 %all-gather.1 = f32[256,1,768]{2,1,0:T(1,128)S(1)} all-gather(f32[1,1,768]{2,1,0:T(1,128)S(1)} %reshape.31), channel_id=1, replica_groups=mesh['vgrp'=4,'samp'=64] {'vgrp','samp'}, dimensions={0}, use_global_device_ids=true | all-gather | bytes 789504 | tf_op jit(solution)/shard_map/all_gather | solution.py:22
  87.5 68.0 %gather_fusion = f32[12288]{0:T(1024)S(1)} fusion(f32[196608]{0:T(1024)S(1)} %bitcast.31, s32[12288]{0:T(1024)S(1)} %broadcast_clamp_fusion), kind=kCustom, calls=%fused_computation | custom fusion | bytes 147456 | tf_op jit(solution)/shard_map/jit(_take)/gather | solution.py:27
  155.7 0.8 fusion.2
  156.6 12.1 %all-gather = f32[3072,16]{0,1:T(8,128)S(1)} all-gather(f32[768,16]{0,1:T(8,128)S(1)} %copy.18), channel_id=2, replica_groups=mesh['vgrp'=4,'samp'=64] {'vgrp'}, dimensions={0}, use_global_device_ids=true | all-gather | bytes 245760 | tf_op jit(solution)/shard_map/all_gather | solution.py:31
  169.2 72.9 %psum.15 = f32[128,16]{0,1:T(8,128)S(1)} all-reduce(f32[128,16]{0,1:T(8,128)S(1)} %fusion.2), channel_id=1, replica_groups=mesh['vgrp'=4,'samp'=64] {'vgrp','samp'}, use_global_device_ids=true, to_apply=%region_3.4 | all-reduce | flops 2048 | bytes 16384 | tf_op jit(solution)/shard_map/psum | solution.py:29
  242.1 14.6 %all-reduce.4.cloned.1.call-done = f32[128,128]{1,0:T(8,128)} async-done(((f32[128,128]{1,0:T(8,128)}), f32[128,128]{1,0:T(8,128)}) %all-reduce.4.cloned.1.call-update) | async-done | bytes 65552 | tf_op jit(solution)/shard_map/psum | solution.py:21
  256.7 1.5 select_add_fusion
  258.2 1.6 copy.19
  259.7 1.5 fusion.11
  261.2 13.2 %cholesky.16 = f32[128,128]{1,0:T(8,128)} custom-call(f32[128,128]{1,0:T(8,128)} %fusion.11), custom_call_target="Cholesky" | custom-call | tf_op jit(solution)/shard_map/jit(cholesky)/cholesky | solution.py:25
  274.4 0.9 select_reduce_fusion
  275.3 0.6 compare_reduce_fusion
  275.9 2.1 fusion.6
  278.0 11.3 %custom-call.8 = f32[1,128,128]{1,2,0:T(8,128)} custom-call(f32[1,128,128]{2,1,0:T(8,128)} %fusion.6), custom_call_target="InvertDiagBlocksLowerTriangular" | custom-call | tf_op jit(solution)/shard_map/triangular_solve | solution.py:9
  289.3 1.0 fusion.9
  290.3 1.0 fusion.7
  291.3 1.4 fusion
  292.8 3.4 multiply_convert_fusion
  296.2 10.8 %convolution_bitcast_fusion.1 = f32[512,2048]{0,1:T(8,128)} fusion(bf16[3072,2048]{0,1:T(8,128)(2,1)S(1)} %bitcast.32, s32[3072,512]{1,0:T(8,128)} %param.7), kind=kOutput, calls=%fused_computation.4 | convolution fusion | flops 6444023808 | bytes 23068672 | tf_op jit(solution)/shard_map/dot_general | solution.py:40
  307.0 0.6 copy-done.2
  308.9 191.7 %all-reduce.6.cloned.1.call-done = f32[512,2048]{0,1:T(8,128)} async-done(((f32[512,2048]{0,1:T(8,128)}), f32[512,2048]{0,1:T(8,128)}) %all-reduce.6.cloned.1.call-update) | async-done | bytes 4194320
  500.6 1.6 dynamic-slice_multiply_fusion
  (20 shorter events, 2.6 us)
Async XLA Ops:
  6.5 2.6 copy-start
  6.5 250.1 %all-reduce.4.cloned.1.call-start = ((), (), s32[]{:S(2)}) async-start(), calls=%async_computation | async-start | bytes 131072 | tf_op jit(solution)/shard_map/psum | solution.py:21
  9.1 491.5 %all-reduce.6.cloned.1.call-start = ((), (), s32[]{:S(2)}) async-start(), calls=%async_computation.1 | async-start | bytes 8388608
  87.5 68.2 %copy-start.1 = (f32[3072,128]{1,0:T(8,128)S(1)}, f32[3072,128]{1,0:T(8,128)}, u32[]{:S(2)}) copy-start(f32[3072,128]{1,0:T(8,128)} %param.5) | copy-start | bytes 4718596
  307.0 0.7 copy-start.2
Sparse Core Ops, SparseCore 0:
  12.8 243.8 all-reduce.3
  307.1 193.4 all-reduce.5
where the time goes:
time: 511 us; the launch traced here: 510 us
  waiting for transfers between devices  206 us (40%)
  blocking collectives  162 us (32%)
  local copies, waits for them, and re-layouts  72.7 us (14%)
  other arithmetic  36.8 us (7%)
  matrix products  17.6 us (3%)
  between operations  14.2 us (3%)
    unnamed x3, waiting for transfers between devices  192 us
    all_gather x1, blocking collectives, per_device(): pheno_full = lax.all_gather(phenotype, ('vgrp', 'samp'), axis=0, tiled=True)  77.2 us
    psum x1, blocking collectives, per_device(): cross = lax.psum(cross_part, ('vgrp', 'samp'))  72.9 us
    gather x3, local copies, waits for them, and re-layouts, per_device(): pheno_part = jnp.take(pheno_full, perm_part.T, axis=0, mode='clip')  68.3 us
    another operation x3, other arithmetic, per_device(): factor = jnp.linalg.cholesky(system)  14.7 us
    psum x1, waiting for transfers between devices, per_device(): gram = lax.psum(gram_part, ('vgrp', 'samp'))  14.6 us
    another operation x2, other arithmetic, chol_solve(): lax.linalg.triangular_solve(factor, middle, left_side=True, lower=True, t...  13.4 us
    all_gather x1, blocking collectives, per_device(): permuted = lax.all_gather(pheno_part, 'vgrp', axis=0, tiled=True)  12.1 us
  transfers between devices with their start and end apart: 2, of which 2 were waited for; matrix products, arithmetic and copies ran while one was open for 14% of the time, Pallas kernels for 0%

commit v1 on v0

--- a/solution.py
+++ b/solution.py
@@ -28,7 +28,27 @@
     cross_part = jnp.dot(expo_part.T, pheno_part, precision=hi)
     cross = lax.psum(cross_part, ("vgrp", "samp"))
     coefficients = chol_solve(factor, cross)
-    permuted = lax.all_gather(pheno_part, "vgrp", axis=0, tiled=True)
+    y1, m_next, y2 = (lax.axis_size("vgrp"), lax.axis_index("vgrp"), pheno_part.shape[0])
+    pages = []
+    for d in range(y1):
+        pages.append((d, (d + 1) % y1))
+    all_rows = []
+    for d in range(y1):
+        all_rows.append((d, (d - 1) % y1))
+    permuted = jnp.zeros((*pheno_part.shape[:0], y1 * y2, *pheno_part.shape[1:]), pheno_part.dtype)
+    kept_arr = res = pheno_part
+    seen_now = y1 // 2
+    permuted = lax.dynamic_update_slice_in_dim(permuted, pheno_part, m_next * y2, axis=0)
+    for t in range(1, seen_now + 1):
+        kept_arr = lax.ppermute(kept_arr, axis_name="vgrp", perm=pages)
+        permuted = lax.dynamic_update_slice_in_dim(
+            permuted, kept_arr, (m_next - t) % y1 * y2, axis=0
+        )
+        if t < y1 - seen_now:
+            res = lax.ppermute(res, "vgrp", perm=all_rows)
+            permuted = lax.dynamic_update_slice_in_dim(
+                permuted, res, (m_next + t) % y1 * y2, axis=0
+            )
     residuals = permuted - jnp.dot(exposures, coefficients, precision=hi)
     nperm = residuals.shape[1]
     weighted = (

time: 511 us -> 655 us (1.28)
  waiting for transfers between devices: 206 us -> 354 us
  blocking collectives: 162 us -> 152 us
    psum x1, waiting for transfers between devices: 14.6 us -> 161 us  [per_device(): gram = lax.psum(gram_part, ('vgrp', 'samp'))]
    all_gather x1 -> x0, blocking collectives: 12.1 us -> none  [per_device(): permuted = lax.all_gather(pheno_part, 'vgrp', axis=0, tiled=True)]
  transfers between devices with their start and end apart: 2 -> 5, of which waited for: 2 -> 3; matrix products, arithmetic and copies ran while one was open for 14% -> 6% of each run, Pallas kernels for 0% -> 0%
where the time goes in v1:
time: 655 us; the launch traced here: 654 us
  waiting for transfers between devices  354 us (54%)
  blocking collectives  152 us (23%)
  local copies, waits for them, and re-layouts  76.7 us (12%)
  other arithmetic  36.8 us (6%)
  matrix products  16.4 us (3%)
  between operations  14.2 us (2%)
    unnamed x3, waiting for transfers between devices  192 us
    psum x1, waiting for transfers between devices, per_device(): gram = lax.psum(gram_part, ('vgrp', 'samp'))  161 us
    all_gather x1, blocking collectives, per_device(): pheno_full = lax.all_gather(phenotype, ('vgrp', 'samp'), axis=0, tiled=True)  77.2 us
    psum x1, blocking collectives, per_device(): cross = lax.psum(cross_part, ('vgrp', 'samp'))  74.8 us
    gather x3, local copies, waits for them, and re-layouts, per_device(): pheno_part = jnp.take(pheno_full, perm_part.T, axis=0, mode='clip')  68.9 us
    another operation x3, other arithmetic, per_device(): factor = jnp.linalg.cholesky(system)  14.7 us
    another operation x2, other arithmetic, chol_solve(): lax.linalg.triangular_solve(factor, middle, left_side=True, lower=True, t...  13.4 us
  transfers between devices with their start and end apart: 5, of which 3 were waited for; matrix products, arithmetic and copies ran while one was open for 6% of the time, Pallas kernels for 0%

profile of v1, /device:TPU:8, one launch (start us, length us, event | category | flops | bytes accessed | tf_op | source)
XLA Modules:
  0.0 654.0 jit_solution(635498410380469955)
XLA Ops:
  6.5 0.9 copy-done
  8.5 77.2 %all-gather = f32[256,1,768]{2,1,0:T(1,128)S(1)} all-gather(f32[1,1,768]{2,1,0:T(1,128)S(1)} %reshape.30), channel_id=1, replica_groups=mesh['vgrp'=4,'samp'=64] {'vgrp','samp'}, dimensions={0}, use_global_device_ids=true | all-gather | bytes 789504 | tf_op jit(solution)/shard_map/all_gather | solution.py:22
  85.7 68.0 %gather_fusion = f32[12288]{0:T(1024)S(1)} fusion(f32[196608]{0:T(1024)S(1)} %bitcast.31, s32[12288]{0:T(1024)S(1)} %broadcast_clamp_fusion), kind=kCustom, calls=%fused_computation | custom fusion | bytes 147456 | tf_op jit(solution)/shard_map/jit(_take)/gather | solution.py:27
  154.7 1.3 collective-permute-start
  156.7 1.4 fusion.4
  160.3 74.8 %psum.15 = f32[128,16]{0,1:T(8,128)S(1)} all-reduce(f32[128,16]{0,1:T(8,128)S(1)} %fusion.2), channel_id=1, replica_groups=mesh['vgrp'=4,'samp'=64] {'vgrp','samp'}, use_global_device_ids=true, to_apply=%region_3.4 | all-reduce | flops 2048 | bytes 16384 | tf_op jit(solution)/shard_map/psum | solution.py:29
  235.1 161.2 %all-reduce.4.cloned.1.call-done = f32[128,128]{1,0:T(8,128)} async-done(((f32[128,128]{1,0:T(8,128)}), f32[128,128]{1,0:T(8,128)}) %all-reduce.4.cloned.1.call-update) | async-done | bytes 65552 | tf_op jit(solution)/shard_map/psum | solution.py:21
  396.3 1.5 select_add_fusion
  397.7 1.6 copy.25
  399.3 1.5 fusion.11
  400.8 13.2 %cholesky.16 = f32[128,128]{1,0:T(8,128)} custom-call(f32[128,128]{1,0:T(8,128)} %fusion.11), custom_call_target="Cholesky" | custom-call | tf_op jit(solution)/shard_map/jit(cholesky)/cholesky | solution.py:25
  414.0 0.9 select_reduce_fusion
  415.5 2.1 fusion.6
  417.6 11.3 %custom-call.8 = f32[1,128,128]{1,2,0:T(8,128)} custom-call(f32[1,128,128]{2,1,0:T(8,128)} %fusion.6), custom_call_target="InvertDiagBlocksLowerTriangular" | custom-call | tf_op jit(solution)/shard_map/triangular_solve | solution.py:9
  428.9 1.0 fusion.9
  429.9 1.0 fusion.7
  430.9 1.7 collective-permute-start.2
  432.7 0.8 constant_dynamic-update-slice_fusion.2
  434.3 1.2 collective-permute-done.2
  435.5 1.4 fusion
  436.9 3.4 multiply_convert_fusion
  440.4 10.8 %convolution_bitcast_fusion.1 = f32[512,2048]{0,1:T(8,128)} fusion(bf16[3072,2048]{0,1:T(8,128)(2,1)S(1)} %bitcast.32, s32[3072,512]{1,0:T(8,128)} %param.7), kind=kOutput, calls=%fused_computation.4 | convolution fusion | flops 6444023808 | bytes 23068672 | tf_op jit(solution)/shard_map/dot_general | solution.py:60
  453.1 191.7 %all-reduce.6.cloned.1.call-done = f32[512,2048]{0,1:T(8,128)} async-done(((f32[512,2048]{0,1:T(8,128)}), f32[512,2048]{0,1:T(8,128)}) %all-reduce.6.cloned.1.call-update) | async-done | bytes 4194320
  644.8 1.6 dynamic-slice_multiply_fusion
  (30 shorter events, 8.3 us)
Async XLA Ops:
  6.5 0.9 copy-start
  6.5 389.7 %all-reduce.4.cloned.1.call-start = ((), (), s32[]{:S(2)}) async-start(), calls=%async_computation | async-start | bytes 131072 | tf_op jit(solution)/shard_map/psum | solution.py:21
  85.7 71.0 %copy-start.1 = (f32[3072,128]{1,0:T(8,128)S(1)}, f32[3072,128]{1,0:T(8,128)}, u32[]{:S(2)}) copy-start(f32[3072,128]{1,0:T(8,128)} %param.5) | copy-start | bytes 4718596
  154.7 276.2 %collective-permute-start = (f32[768,16]{0,1:T(8,128)}, f32[768,16]{0,1:T(8,128)}, u32[]{:S(2)}, u32[]{:S(2)}) collective-permute-start(f32[768,16]{0,1:T(8,128)} %copy.22), channel_id=1, source_target_pairs={{0,64},{64,128},{128,192},{192,0},{1,65},{65,129},{129,193},{193,1... | collective-permute-start | bytes 147464 | tf_op jit(solution)/shard_map/ppermute | solution.py:43
  155.9 277.6 %collective-permute-start.1 = (f32[768,16]{0,1:T(8,128)}, f32[768,16]{0,1:T(8,128)}, u32[]{:S(2)}, u32[]{:S(2)}) collective-permute-start(f32[768,16]{0,1:T(8,128)} %copy.22), channel_id=1, source_target_pairs={{0,192},{64,0},{128,64},{192,128},{1,193},{65,1},{129,65},{193,129... | collective-permute-start | bytes 147464 | tf_op jit(solution)/shard_map/ppermute | solution.py:48
  158.1 486.6 %all-reduce.6.cloned.1.call-start = ((), (), s32[]{:S(2)}) async-start(), calls=%async_computation.1 | async-start | bytes 8388608
  430.9 4.6 collective-permute-start.2
  451.2 0.7 copy-start.2
Sparse Core Ops, SparseCore 0:
  158.3 237.9 all-reduce.3
  451.3 193.3 all-reduce.5

commit v2 on v0

--- a/solution.py
+++ b/solution.py
@@ -26,7 +26,8 @@
     perm_part = lax.dynamic_slice_in_dim(perms, offset_rows, quarter, 1)
     pheno_part = jnp.take(pheno_full, perm_part.T, axis=0, mode="clip")
     cross_part = jnp.dot(expo_part.T, pheno_part, precision=hi)
-    cross = lax.psum(cross_part, ("vgrp", "samp"))
+    terms = lax.all_gather(cross_part, ("vgrp", "samp"), axis=0, tiled=False)
+    cross = terms.sum(axis=0)
     coefficients = chol_solve(factor, cross)
     permuted = lax.all_gather(pheno_part, "vgrp", axis=0, tiled=True)
     residuals = permuted - jnp.dot(exposures, coefficients, precision=hi)

time: 511 us -> 584 us (1.14)
  waiting for transfers between devices: 206 us -> 360 us
  blocking collectives: 162 us -> 89.5 us
  other arithmetic: 36.8 us -> 30.7 us
    all_gather x0 -> x1, waiting for transfers between devices: none -> 81.3 us  [per_device(): terms = lax.all_gather(cross_part, ('vgrp', 'samp'), axis=0, tiled=False)]
    psum x1 -> x0, blocking collectives: 72.9 us -> none  [per_device(): cross = lax.psum(cross_part, ('vgrp', 'samp'))]
    psum x1, waiting for transfers between devices: 14.6 us -> 85.5 us  [per_device(): gram = lax.psum(gram_part, ('vgrp', 'samp'))]
    unnamed x3 -> x4, waiting for transfers between devices: 192 us -> 194 us
  transfers between devices with their start and end apart: 2 -> 3, of which waited for: 2 -> 3; matrix products, arithmetic and copies ran while one was open for 14% -> 17% of each run, Pallas kernels for 0% -> 0%
where the time goes in v2:
time: 584 us
  waiting for transfers between devices  360 us (62%)
  blocking collectives  89.5 us (15%)
  local copies, waits for them, and re-layouts  74.5 us (13%)
  other arithmetic  30.7 us (5%)
  matrix products  14.6 us (2%)
  between operations  13.9 us (2%)
    unnamed x4, waiting for transfers between devices  194 us
    psum x1, waiting for transfers between devices, per_device(): gram = lax.psum(gram_part, ('vgrp', 'samp'))  85.5 us
    all_gather x1, waiting for transfers between devices, per_device(): terms = lax.all_gather(cross_part, ('vgrp', 'samp'), axis=0, tiled=False)  81.3 us
    all_gather x1, blocking collectives, per_device(): pheno_full = lax.all_gather(phenotype, ('vgrp', 'samp'), axis=0, tiled=True)  77.2 us
    gather x3, local copies, waits for them, and re-layouts, per_device(): pheno_part = jnp.take(pheno_full, perm_part.T, axis=0, mode='clip')  68.3 us
    another operation x3, other arithmetic, per_device(): factor = jnp.linalg.cholesky(system)  12.4 us
    all_gather x1, blocking collectives, per_device(): permuted = lax.all_gather(pheno_part, 'vgrp', axis=0, tiled=True)  12.3 us
  transfers between devices with their start and end apart: 3, of which 3 were waited for; matrix products, arithmetic and copies ran while one was open for 17% of the time, Pallas kernels for 0%

profile of v2, /device:TPU:8, one launch (start us, length us, event | category | flops | bytes accessed | tf_op | source)
XLA Modules:
  0.0 583.7 jit_solution(15229395256537473135)
XLA Ops:
  6.5 2.6 fusion.4
  9.6 0.7 reshape.32
  10.2 77.2 %all-gather.2 = f32[256,1,768]{2,1,0:T(1,128)S(1)} all-gather(f32[1,1,768]{2,1,0:T(1,128)S(1)} %reshape.32), channel_id=1, replica_groups=mesh['vgrp'=4,'samp'=64] {'vgrp','samp'}, dimensions={0}, use_global_device_ids=true | all-gather | bytes 789504 | tf_op jit(solution)/shard_map/all_gather | solution.py:22
  87.4 68.0 %gather_fusion = f32[12288]{0:T(1024)S(1)} fusion(f32[196608]{0:T(1024)S(1)} %bitcast.36, s32[12288]{0:T(1024)S(1)} %broadcast_clamp_fusion), kind=kCustom, calls=%fused_computation | custom fusion | bytes 147456 | tf_op jit(solution)/shard_map/jit(_take)/gather | solution.py:27
  155.7 1.4 fusion.2
  157.2 1.6 copy.16
  158.9 12.3 %all-gather = f32[3072,16]{0,1:T(8,128)S(1)} all-gather(f32[768,16]{0,1:T(8,128)S(1)} %copy.18), channel_id=2, replica_groups=mesh['vgrp'=4,'samp'=64] {'vgrp'}, dimensions={0}, use_global_device_ids=true | all-gather | bytes 245760 | tf_op jit(solution)/shard_map/all_gather | solution.py:32
  171.2 85.5 %all-reduce.4.cloned.1.call-done = f32[128,128]{1,0:T(8,128)} async-done(((f32[128,128]{1,0:T(8,128)}), f32[128,128]{1,0:T(8,128)}) %all-reduce.4.cloned.1.call-update) | async-done | bytes 65552 | tf_op jit(solution)/shard_map/psum | solution.py:21
  256.6 0.9 select_add_fusion
  257.6 0.9 fusion.11
  258.4 11.7 %cholesky.16 = f32[128,128]{1,0:T(8,128)S(1)} custom-call(f32[128,128]{1,0:T(8,128)S(1)} %fusion.11), custom_call_target="Cholesky" | custom-call | tf_op jit(solution)/shard_map/jit(cholesky)/cholesky | solution.py:25
  270.2 0.6 compare_reduce_fusion
  270.8 0.7 fusion.6
  271.5 9.8 %custom-call.8 = f32[1,128,128]{1,2,0:T(8,128)S(1)} custom-call(f32[1,128,128]{2,1,0:T(8,128)S(1)} %fusion.6), custom_call_target="InvertDiagBlocksLowerTriangular" | custom-call | tf_op jit(solution)/shard_map/triangular_solve | solution.py:9
  281.3 81.3 %all-gather.5.cloned.1.call-done = f32[32768,16]{0,1:T(8,128)} async-done(((f32[128,16]{0,1:T(8,128)}), f32[32768,16]{0,1:T(8,128)}) %all-gather.5.cloned.1.call-update) | async-done | bytes 2097168 | tf_op jit(solution)/shard_map/all_gather | solution.py:29
  362.6 2.1 copy.23
  365.2 1.4 fusion
  366.7 3.7 multiply_convert_fusion
  370.5 8.9 %convolution_bitcast_fusion.1 = f32[512,2048]{0,1:T(8,128)} fusion(bf16[3072,2048]{0,1:T(8,128)(2,1)S(1)} %bitcast.37, s32[3072,512]{1,0:T(8,128)S(1)} %bitcast.41), kind=kOutput, calls=%fused_computation.4 | convolution fusion | flops 6444023808 | bytes 23068672 | tf_op jit(solution)/shard_map/dot_general | solution.py:41
  379.4 0.6 copy-done.3
  380.1 0.6 dynamic-slice
  381.3 193.5 %all-reduce.6.cloned.1.call-done = f32[512,2048]{0,1:T(8,128)} async-done(((f32[512,2048]{0,1:T(8,128)}), f32[512,2048]{0,1:T(8,128)}) %all-reduce.6.cloned.1.call-update) | async-done | bytes 4194320
  574.8 1.6 dynamic-slice_multiply_fusion
  576.6 0.6 broadcast_multiply_fusion
  (31 shorter events, 1.6 us)
Async XLA Ops:
  6.5 2.6 copy-start
  6.5 250.1 %all-reduce.4.cloned.1.call-start = ((), (), s32[]{:S(2)}) async-start(), calls=%async_computation | async-start | bytes 131072 | tf_op jit(solution)/shard_map/psum | solution.py:21
  9.1 353.5 %all-gather.5.cloned.1.call-start = ((), (), s32[]{:S(2)}) async-start(), calls=%async_computation.1 | async-start | bytes 2105344 | tf_op jit(solution)/shard_map/all_gather | solution.py:29
  87.4 68.2 %copy-start.1 = (f32[3072,128]{1,0:T(8,128)S(1)}, f32[3072,128]{1,0:T(8,128)}, u32[]{:S(2)}) copy-start(f32[3072,128]{1,0:T(8,128)} %param.5) | copy-start | bytes 4718596
  157.1 417.7 %all-reduce.6.cloned.1.call-start = ((), (), s32[]{:S(2)}) async-start(), calls=%async_computation.2 | async-start | bytes 8388608
  362.6 4.1 copy-start.2
  362.6 7.8 %slice-start = ((s8[6291456]{0:T(1024)(128)(4,1)}), s8[4194304]{0:T(1024)(128)(4,1)S(1)}, s32[]{:S(2)}) async-start(s8[6291456]{0:T(1024)(128)(4,1)} %bitcast.40), calls=%async_computation.3 | async-start | bytes 8388608
  366.7 3.7 slice-start.1
  379.4 0.7 copy-start.3
Sparse Core Ops, SparseCore 0:
  12.8 243.7 all-reduce.3
  260.4 102.1 all-gather.4
  379.5 195.2 all-reduce.5
